TPU v7x, 32 devices: a whole 2x2x4 slice. The times are simulated.
32 devices in a mesh: region: 4 (over z), narrow: 8 (over y, x, core).
Axes of the slice: x: 2, y: 2, z: 4, core: 2. Of those that a mesh axis runs over, the one named last changes fastest.
Arguments:
- dust_pos: float32 [3, 6144], P(None, ('region', 'narrow')), may hold values from -1 to 1
- dust_vel: float32 [3, 6144], P(None, ('region', 'narrow')), may hold values from -6 to 6
- dust_tau: float32 [6144], P(('region', 'narrow')), may hold values from 0.02 to 2
- dest: int32 [6144, 1], P(('region', 'narrow')), may hold values from 0 to 3; in each aligned block of 192 rows (0 to 191, 192 to 383, ...) at most 96 rows name the same one
- counts: int32 [32], P(('region', 'narrow')), may hold values from 96 to 192, as said below
- wake_pos: float32 [3, 32768], P(None, ('region', 'narrow')), may hold values from -1 to 1
- wake_gamma: float32 [3, 32768], P(None, ('region', 'narrow')), may hold values from -0.3 to 0.3
- wake_core: float32 [32768], P(('region', 'narrow')), may hold values from 0.05 to 0.3
Outputs:
- moved: float32 [6, 12288], P(None, ('region', 'narrow'))
Inputs may be any that keep to these rules, and one draw needn't show every extreme that they name: `dest`: in each device's 192 rows, no region is named by more than 96 rows, and some device's rows name some region exactly 96 times. `counts`: some device has all its rows live in every draw.
All inputs are finite; a program needn't handle non-finite values.
Results may differ from a plain program's by a relative error of at most 0.0003.
Values sent between devices are 32-bit elements; how exact they have to be, the bound alone decides.
No kernel may reach another device: no remote copies, remote signals or barrier semaphores. Data moves between devices by JAX's collectives and lax.ppermute only.
A program may use at most 64 MiB of HBM per device.

v0:
```python
import math
import jax
import jax.numpy as jnp
from jax import lax
from jax.sharding import PartitionSpec as P

step_size = 0.1
gravity = 1.0


def cross_rows(first, second):
    return jnp.stack(
        [
            first[1] * second[2] - first[2] * second[1],
            first[2] * second[0] - first[0] * second[2],
            first[0] * second[1] - first[1] * second[0],
        ]
    )


def raw_terms(points, wake_block):
    point_count = points.shape[1]
    wake_count = wake_block.shape[1]
    wake_width = math.gcd(wake_count, 2048)
    wake_place = wake_block[0:3]
    vortex_gamma = wake_block[3:6]
    core_square = wake_block[6] * wake_block[6]
    tables = jnp.concatenate([vortex_gamma, cross_rows(vortex_gamma, wake_place)], axis=0)
    place_blocks = wake_place.reshape(3, wake_count // wake_width, wake_width).transpose(1, 0, 2)
    table_blocks = tables.reshape(6, wake_count // wake_width, wake_width).transpose(1, 0, 2)
    core_blocks = core_square.reshape(wake_count // wake_width, wake_width)
    point_blocks = points.reshape(3, point_count // point_count, point_count).transpose(1, 0, 2)

    def one_block(point_group):

        def accumulate(running, parts):
            place_part, table_part, core_part = parts
            first_gap = point_group[0][:, None] - place_part[0][None, :]
            second_gap = point_group[1][:, None] - place_part[1][None, :]
            third_gap = point_group[2][:, None] - place_part[2][None, :]
            distance_sq = (
                first_gap * first_gap
                + second_gap * second_gap
                + third_gap * third_gap
                + core_part[None, :]
            )
            kernel = 1.0 / (distance_sq * jnp.sqrt(distance_sq))
            product = lax.dot_general(
                table_part, kernel, (((1,), (1,)), ((), ())), precision=lax.Precision.HIGHEST
            )
            return (running + product, None)

        total, _ = lax.scan(
            accumulate,
            jnp.zeros((6, point_count), jnp.float32),
            (place_blocks, table_blocks, core_blocks),
        )
        return total

    result = lax.map(one_block, point_blocks)
    return result.transpose(1, 0, 2).reshape(6, point_count)


def advance(arrived, raw_sums):
    points = arrived[0:3]
    velocity = arrived[3:6]
    live_flag = arrived[7]
    wind = (cross_rows(raw_sums[0:3], points) - raw_sums[3:6]) / (4.0 * math.pi)
    safe_tau = jnp.where(live_flag > 0.5, arrived[6], 1.0)
    rate = step_size / safe_tau
    upward = jnp.array([0.0, 0.0, 1.0], jnp.float32)[:, None]
    new_velocity = (velocity + rate[None, :] * wind - step_size * gravity * upward) / (
        1.0 + rate[None, :]
    )
    new_place = points + step_size * new_velocity
    return jnp.concatenate([new_place, new_velocity], axis=0) * live_flag[None, :]


def body(dust_pos, dust_vel, dust_tau, dest, counts, wake_pos, wake_gamma, wake_core):
    per_device = dust_tau.shape[0]
    regions = lax.axis_size("region")
    capacity = 2 * per_device // regions
    slot_count = regions * capacity
    live_rows = (jnp.arange(per_device, dtype=jnp.int32) < counts[0]).astype(jnp.float32)
    target = dest[:, 0]
    onehot = (target[:, None] == jnp.arange(regions, dtype=jnp.int32)[None, :]).astype(jnp.int32)
    slot_rank = jnp.sum((jnp.cumsum(onehot, axis=0) - onehot) * onehot, axis=1)
    column = target * capacity + slot_rank
    placing = (column[:, None] == jnp.arange(slot_count, dtype=jnp.int32)[None, :]).astype(
        jnp.float32
    )
    dust_state = (
        jnp.concatenate(
            [dust_pos, dust_vel, dust_tau[None, :], jnp.ones((1, per_device), jnp.float32)], axis=0
        )
        * live_rows[None, :]
    )
    outgoing = jnp.dot(
        dust_state, placing, precision=lax.Precision.HIGHEST, preferred_element_type=jnp.float32
    )
    arrived = lax.all_to_all(outgoing, "region", split_axis=1, concat_axis=1, tiled=True)
    points = arrived[0:3]
    wake_rows = jnp.concatenate([wake_pos, wake_gamma, wake_core[None, :]], axis=0)
    raw_sums = raw_terms(points, lax.all_gather(wake_rows, "narrow", axis=1, tiled=True))
    return advance(arrived, raw_sums)


def solution(mesh):
    in_specs = (
        P(None, ("region", "narrow")),
        P(None, ("region", "narrow")),
        P(("region", "narrow")),
        P(("region", "narrow"), None),
        P(("region", "narrow")),
        P(None, ("region", "narrow")),
        P(None, ("region", "narrow")),
        P(("region", "narrow")),
    )
    out_specs = P(None, ("region", "narrow"))
    return jax.shard_map(body, mesh=mesh, in_specs=in_specs, out_specs=out_specs, check_vma=False)
```

profile of v0, /device:TPU:0, one launch (start us, length us, event | category | flops | bytes accessed | tf_op | source)
XLA Modules:
  0.0 41.4 jit_solution(17835298949323918834)
XLA Ops:
  0.0 0.0 copy-start.2
  0.0 0.0 copy-start.1
  0.0 0.0 copy-start
  0.0 0.7 %iota_compare_fusion.2 = pred[4,192]{1,0:T(4,128)(4,1)S(1)} fusion(s32[192]{0:T(256)} %bitcast.53), kind=kLoop, calls=%fused_computation.52 | loop fusion | flops 768 | bytes 1536 | tf_op jit(solution)/shard_map/eq | solution.py:86
  0.7 1.2 %reduce-window.6 = s32[4,2,128]{2,1,0:T(2,128)S(1)} reduce-window(s32[4,2,128]{2,1,0:T(2,128)S(1)} %reshape.73, s32[]{:T(128)} %constant.25.clone.1), window={size=1x1x128 pad=0_0x0_0x127_0}, to_apply=%region_0.0 | reduce-window | flops 130048 | bytes 8196 | tf_op jit(solution)/shard_map/reduce-window
  2.0 0.1 slice.176
  2.0 0.1 copy.15
  2.2 0.1 copy.16
  2.3 0.1 add_bitcast_fusion
  2.4 0.7 %fusion.31 = s32[192]{0:T(256)S(1)} fusion(s32[256,4]{0,1:T(4,128)S(1)} %bitcast.52, s32[192]{0:T(256)} %bitcast.54), kind=kLoop, calls=%fused_computation.49 | loop fusion | flops 3648 | bytes 4608 | tf_op jit(solution)/shard_map/reduce_sum | solution.py:87
  3.1 0.7 %multiply_add_fusion.1 = s32[192,1]{0,1:T(1,128)S(1)} fusion(s32[192,1]{0,1:T(1,128)S(1)} %bitcast.57, s32[192,1]{0,1:T(1,128)} %param.14), kind=kLoop, calls=%fused_computation.68 | loop fusion | flops 384 | bytes 2304 | tf_op jit(solution)/shard_map/add | solution.py:88
  4.4 0.1 pad.20.clone
  4.5 1.0 %fusion.18 = f32[8,384]{1,0:T(8,128)S(1)} fusion(s32[192]{0:T(256)S(1)} %bitcast.58, f32[1,192]{1,0:T(1,128)} %bitcast.59, f32[3,192]{1,0:T(4,128)} %param.12, f32[3,192]{1,0:T(4,128)} %param.11, f32[8]{0:T(128)S(1)} %pad.20.clone, f32[192]{0:T(256)S(1)} %compare_convert_fusion), kind=kOutput, calls=%fused_computation.24 | convolution fusion | flops 7157760 | bytes 19232 | tf_op jit(solution)/shard_map/dot_general | solution.py:98
  5.5 0.1 all_to_all.6
  5.6 0.6 %copy.17 = f32[8,4,96]{2,0,1:T(8,128)} copy(f32[8,4,96]{2,1,0:T(4,128)S(1)} %all_to_all.6) | data formatting | bytes 24576 | tf_op jit(solution)/shard_map/all_to_all | solution.py:101
  6.2 6.3 %all-to-all-start = ((f32[8,4,96]{2,0,1:T(8,128)}), f32[8,4,96]{2,0,1:T(8,128)S(1)}, u32[]{:S(2)}, u32[]{:S(2)}) async-start(f32[8,4,96]{2,0,1:T(8,128)} %copy.17), calls=%async_computation | async-start | bytes 32768 | tf_op jit(solution)/shard_map/all_to_all | solution.py:101
  12.5 0.0 copy-done.2
  12.5 0.0 copy-done.1
  12.5 0.0 copy-done
  12.5 9.3 %all_gather.3 = f32[7,8192]{1,0:T(8,128)S(1)} all-gather(f32[7,1024]{1,0:T(8,128)S(1)} %pad_maximum_fusion), channel_id=1, replica_groups=mesh['region'=4,'narrow'=8] {'narrow'}, dimensions={1}, use_global_device_ids=true | all-gather | bytes 258048 | tf_op jit(solution)/shard_map/all_gather | solution.py:104
  21.9 0.3 fusion.20
  22.1 0.1 fusion.36
  22.2 0.1 maximum_bitcast_fusion
  22.3 0.0 all-to-all-done
  22.4 0.1 slice.144
  22.5 0.0 copy-start.3
  22.5 17.6 %while.18 = (s32[]{:T(128)}, f32[6,384]{1,0:T(8,128)S(1)}, f32[4,6,2048]{2,1,0:T(8,128)S(1)}, f32[3,384]{1,0:T(4,128)S(1)}, f32[4,3,2048]{2,1,0:T(4,128)S(1)}, /...) while((s32[]{:T(128)}, f32[6,384]{1,0:T(8,128)S(1)}, ...), condition=%wide.region_4.5_spmd.clone, body=%wide.region_3.4_spmd.clone.sunk | while | flops 65278468 | bytes 200859 | solution.py:53
  22.6 4.3 %fusion.43 = f32[6,384]{1,0:T(8,128)S(1)} fusion(f32[2048]{0:T(1024)S(1)} %bitcast.48, f32[2048]{0:T(1024)S(1)} %bitcast.47, f32[384]{0:T(512)S(1)} %get-tuple-element.159, f32[2048]{0:T(1024)S(1)} %bitcast.46, f32[384]{0:T(512)S(1)} %get-tuple-element.161, f32[2048]{0:T(1024)S(1)} %bitcast.45, f32[384]{0:T(512)S(1)} %get-tuple-element.163, ...), kind=kOutput, calls=%fused_computation.11.clone.1 | convolution fusion | flops 65278464 | bytes 125957 | tf_op jit(solution)/shard_map/while/body/eval_jaxpr/while/body/eval_jaxpr/dot_general | solution.py:48
  27.0 4.3 %fusion.43 = f32[6,384]{1,0:T(8,128)S(1)} fusion(f32[2048]{0:T(1024)S(1)} %bitcast.48, f32[2048]{0:T(1024)S(1)} %bitcast.47, f32[384]{0:T(512)S(1)} %get-tuple-element.159, f32[2048]{0:T(1024)S(1)} %bitcast.46, f32[384]{0:T(512)S(1)} %get-tuple-element.161, f32[2048]{0:T(1024)S(1)} %bitcast.45, f32[384]{0:T(512)S(1)} %get-tuple-element.163, ...), kind=kOutput, calls=%fused_computation.11.clone.1 | convolution fusion | flops 65278464 | bytes 125957 | tf_op jit(solution)/shard_map/while/body/eval_jaxpr/while/body/eval_jaxpr/dot_general | solution.py:48
  31.4 4.3 %fusion.43 = f32[6,384]{1,0:T(8,128)S(1)} fusion(f32[2048]{0:T(1024)S(1)} %bitcast.48, f32[2048]{0:T(1024)S(1)} %bitcast.47, f32[384]{0:T(512)S(1)} %get-tuple-element.159, f32[2048]{0:T(1024)S(1)} %bitcast.46, f32[384]{0:T(512)S(1)} %get-tuple-element.161, f32[2048]{0:T(1024)S(1)} %bitcast.45, f32[384]{0:T(512)S(1)} %get-tuple-element.163, ...), kind=kOutput, calls=%fused_computation.11.clone.1 | convolution fusion | flops 65278464 | bytes 125957 | tf_op jit(solution)/shard_map/while/body/eval_jaxpr/while/body/eval_jaxpr/dot_general | solution.py:48
  35.8 4.3 %fusion.43 = f32[6,384]{1,0:T(8,128)S(1)} fusion(f32[2048]{0:T(1024)S(1)} %bitcast.48, f32[2048]{0:T(1024)S(1)} %bitcast.47, f32[384]{0:T(512)S(1)} %get-tuple-element.159, f32[2048]{0:T(1024)S(1)} %bitcast.46, f32[384]{0:T(512)S(1)} %get-tuple-element.161, f32[2048]{0:T(1024)S(1)} %bitcast.45, f32[384]{0:T(512)S(1)} %get-tuple-element.163, ...), kind=kOutput, calls=%fused_computation.11.clone.1 | convolution fusion | flops 65278464 | bytes 125957 | tf_op jit(solution)/shard_map/while/body/eval_jaxpr/while/body/eval_jaxpr/dot_general | solution.py:48
  40.1 0.1 slice_reduce_fusion.4
  40.1 0.1 slice.158
  40.2 0.1 slice.161
  40.3 0.1 slice.163
  40.4 0.1 slice.167
  40.4 0.1 slice.169
  40.6 0.1 slice.146
  40.7 0.0 copy-done.3
  40.7 0.1 multiply_add_fusion
  40.7 0.6 %maximum_multiply_fusion = f32[6,384]{1,0:T(8,128)} fusion(f32[3,384]{1,0:T(4,128)S(1)} %get-tuple-element.98, f32[3,384]{1,0:T(4,128)S(1)} %get-tuple-element.97, f32[384]{0:T(512)S(1)} %slice.167), kind=kLoop, calls=%fused_computation.33 | loop fusion | flops 4608 | bytes 19968 | tf_op jit(solution)/shard_map/mul | solution.py:76
  (27 shorter events, 0.4 us)
Async XLA Ops:
  0.0 12.5 %copy-start.2 = (f32[1024]{0:T(1024)S(1)}, f32[1024]{0:T(1024)}, u32[]{:S(2)}) copy-start(f32[1024]{0:T(1024)} %param.18) | copy-start | bytes 12292
  0.0 12.5 %copy-start.1 = (f32[3,1024]{1,0:T(4,128)S(1)}, f32[3,1024]{1,0:T(4,128)}, u32[]{:S(2)}) copy-start(f32[3,1024]{1,0:T(4,128)} %param.16) | copy-start | bytes 36868
  0.0 12.5 %copy-start = (f32[3,1024]{1,0:T(4,128)S(1)}, f32[3,1024]{1,0:T(4,128)}, u32[]{:S(2)}) copy-start(f32[3,1024]{1,0:T(4,128)} %param.17) | copy-start | bytes 36868
  6.2 16.2 %all-to-all-start = ((f32[8,4,96]{2,0,1:T(8,128)}), f32[8,4,96]{2,0,1:T(8,128)S(1)}, u32[]{:S(2)}, u32[]{:S(2)}) async-start(f32[8,4,96]{2,0,1:T(8,128)} %copy.17), calls=%async_computation | async-start | bytes 32768 | tf_op jit(solution)/shard_map/all_to_all | solution.py:101
  22.5 18.2 %copy-start.3 = (f32[3]{0:T(128)S(1)}, f32[3]{0:T(128)}, u32[]{:S(2)}) copy-start(f32[3]{0:T(128)} %constant.56) | copy-start | bytes 40
where the time goes:
time: 41.7 us; the launch traced here: 41.4 us
  matrix products  18.2 us (44%)
  blocking collectives  9.32 us (22%)
  starting transfers between devices  6.33 us (15%)
  other arithmetic  4.56 us (11%)
  local copies, waits for them, and re-layouts  2.08 us (5%)
  between operations  0.78 us (2%)
    dot_general x4, matrix products, accumulate(): lax.dot_general(table_part, kernel, (((1,), (1,)), ((), ())), precision=l...  17.2 us
    all_gather x1, blocking collectives, body(): lax.all_gather(wake_rows, 'narrow', axis=1, tiled=True)  9.32 us
    all_to_all x1, starting transfers between devices, body(): lax.all_to_all(outgoing, 'region', split_axis=1, concat_axis=1, tiled=True)  6.33 us
    another operation x3, other arithmetic  1.26 us
    dot_general x1, matrix products, body(): jnp.dot(dust_state, placing, precision=lax.Precision.HIGHEST, preferred_e...  0.99 us
  transfers between devices with their start and end apart: 1, of which 0 were waited for; matrix products, arithmetic and copies ran while one was open for 1% of the time, Pallas kernels for 0%

commit v1 on v0

--- a/solution.py
+++ b/solution.py
@@ -6,6 +6,24 @@
 
 step_size = 0.1
 gravity = 1.0
+
+
+def collect(shard, axis, dim):
+    ways, here, step = (lax.axis_size(axis), lax.axis_index(axis), shard.shape[dim])
+    lengths = [n * ways if d == dim else n for d, n in enumerate(shard.shape)]
+    full = lax.dynamic_update_slice_in_dim(
+        jnp.zeros(lengths, shard.dtype), shard, here * step, axis=dim
+    )
+    going_up = going_down = shard
+    for far in range(1, ways // 2 + 1):
+        going_up = lax.ppermute(going_up, axis, [(d, (d + 1) % ways) for d in range(ways)])
+        full = lax.dynamic_update_slice_in_dim(full, going_up, (here - far) % ways * step, axis=dim)
+        if 2 * far < ways:
+            going_down = lax.ppermute(going_down, axis, [(d, (d - 1) % ways) for d in range(ways)])
+            full = lax.dynamic_update_slice_in_dim(
+                full, going_down, (here + far) % ways * step, axis=dim
+            )
+    return full
 
 
 def cross_rows(first, second):
@@ -101,7 +119,7 @@
     arrived = lax.all_to_all(outgoing, "region", split_axis=1, concat_axis=1, tiled=True)
     points = arrived[0:3]
     wake_rows = jnp.concatenate([wake_pos, wake_gamma, wake_core[None, :]], axis=0)
-    raw_sums = raw_terms(points, lax.all_gather(wake_rows, "narrow", axis=1, tiled=True))
+    raw_sums = raw_terms(points, collect(wake_rows, "narrow", 1))
     return advance(arrived, raw_sums)
 
 

time: 41.7 us -> 50.7 us (1.22)
  waiting for transfers between devices: 0.01 us -> 10.2 us
  blocking collectives: 9.32 us -> 0 us
  starting transfers between devices: 6.33 us -> 14.3 us
    all_gather x1 -> x0, blocking collectives: 9.32 us -> none  [body(): lax.all_gather(wake_rows, 'narrow', axis=1, tiled=True)]
    ppermute x0 -> x7, starting transfers between devices: none -> 8.02 us  [the longest x3 7.9 us: collect(): lax.ppermute(going_down, axis, [(d, (d - 1) % ways) for d in range(ways)])]
    ppermute x0 -> x7, waiting for transfers between devices: none -> 7.36 us  [the longest x4 7.35 us: collect(): lax.ppermute(going_up, axis, [(d, (d + 1) % ways) for d in range(ways)])]
    all_to_all x1, waiting for transfers between devices: 0.01 us -> 2.83 us  [body(): lax.all_to_all(outgoing, 'region', split_axis=1, concat_axis=1, tiled=True)]
  transfers between devices with their start and end apart: 1 -> 8, of which waited for: 0 -> 4; matrix products, arithmetic and copies ran while one was open for 1% -> 1% of each run, Pallas kernels for 0% -> 0%
where the time goes in v1:
time: 50.7 us; the launch traced here: 50.4 us
  matrix products  18.2 us (36%)
  starting transfers between devices  14.3 us (28%)
  waiting for transfers between devices  10.2 us (20%)
  other arithmetic  4.58 us (9%)
  local copies, waits for them, and re-layouts  2.14 us (4%)
  between operations  0.84 us (2%)
    dot_general x4, matrix products, accumulate(): lax.dot_general(table_part, kernel, (((1,), (1,)), ((), ())), precision=l...  17.2 us
    ppermute x3, starting transfers between devices, collect(): lax.ppermute(going_down, axis, [(d, (d - 1) % ways) for d in range(ways)])  7.9 us
    ppermute x4, waiting for transfers between devices, collect(): lax.ppermute(going_up, axis, [(d, (d + 1) % ways) for d in range(ways)])  7.35 us
    all_to_all x1, starting transfers between devices, body(): lax.all_to_all(outgoing, 'region', split_axis=1, concat_axis=1, tiled=True)  6.32 us
    all_to_all x1, waiting for transfers between devices, body(): lax.all_to_all(outgoing, 'region', split_axis=1, concat_axis=1, tiled=True)  2.83 us
    another operation x3, other arithmetic  1.26 us
  transfers between devices with their start and end apart: 8, of which 4 were waited for; matrix products, arithmetic and copies ran while one was open for 1% of the time, Pallas kernels for 0%

profile of v1, /device:TPU:0, one launch (start us, length us, event | category | flops | bytes accessed | tf_op | source)
XLA Modules:
  0.0 50.4 jit_solution(15386574969976524291)
XLA Ops:
  0.0 0.7 %iota_compare_fusion.2 = pred[4,192]{1,0:T(4,128)(4,1)S(1)} fusion(s32[192]{0:T(256)} %bitcast.53), kind=kLoop, calls=%fused_computation.52 | loop fusion | flops 768 | bytes 1536 | tf_op jit(solution)/shard_map/eq | solution.py:104
  0.7 1.2 %reduce-window.6 = s32[4,2,128]{2,1,0:T(2,128)S(1)} reduce-window(s32[4,2,128]{2,1,0:T(2,128)S(1)} %reshape.73, s32[]{:T(128)} %constant.94.clone.1), window={size=1x1x128 pad=0_0x0_0x127_0}, to_apply=%region_0.0 | reduce-window | flops 130048 | bytes 8196 | tf_op jit(solution)/shard_map/reduce-window
  1.9 0.1 slice.176
  2.0 0.1 copy.15
  2.2 0.1 copy.16
  2.2 0.1 add_bitcast_fusion
  2.3 0.7 %fusion.31 = s32[192]{0:T(256)S(1)} fusion(s32[256,4]{0,1:T(4,128)S(1)} %bitcast.52, s32[192]{0:T(256)} %bitcast.54), kind=kLoop, calls=%fused_computation.49 | loop fusion | flops 3648 | bytes 4608 | tf_op jit(solution)/shard_map/reduce_sum | solution.py:105
  3.1 0.7 %multiply_add_fusion.1 = s32[192,1]{0,1:T(1,128)S(1)} fusion(s32[192,1]{0,1:T(1,128)S(1)} %bitcast.57, s32[192,1]{0,1:T(1,128)} %param.14), kind=kLoop, calls=%fused_computation.76 | loop fusion | flops 384 | bytes 2304 | tf_op jit(solution)/shard_map/add | solution.py:106
  4.4 0.1 pad.20.clone
  4.5 1.0 %fusion.18 = f32[8,384]{1,0:T(8,128)S(1)} fusion(s32[192]{0:T(256)S(1)} %bitcast.58, f32[1,192]{1,0:T(1,128)} %bitcast.59, f32[3,192]{1,0:T(4,128)} %param.12, f32[3,192]{1,0:T(4,128)} %param.11, f32[8]{0:T(128)S(1)} %pad.20.clone, f32[192]{0:T(256)S(1)} %compare_convert_fusion), kind=kOutput, calls=%fused_computation.24 | convolution fusion | flops 7157760 | bytes 19232 | tf_op jit(solution)/shard_map/dot_general | solution.py:116
  5.5 0.1 all_to_all.6
  5.6 0.6 %copy.17 = f32[8,4,96]{2,0,1:T(8,128)} copy(f32[8,4,96]{2,1,0:T(4,128)S(1)} %all_to_all.6) | data formatting | bytes 24576 | tf_op jit(solution)/shard_map/all_to_all | solution.py:119
  6.2 6.3 %all-to-all-start = ((f32[8,4,96]{2,0,1:T(8,128)}), f32[8,4,96]{2,0,1:T(8,128)S(1)}, u32[]{:S(2)}, u32[]{:S(2)}) async-start(f32[8,4,96]{2,0,1:T(8,128)} %copy.17), calls=%async_computation | async-start | bytes 32768 | tf_op jit(solution)/shard_map/all_to_all | solution.py:119
  12.5 0.0 copy-done
  12.6 0.1 collective-permute-start
  12.6 2.6 %collective-permute-start.1 = (f32[7,1024]{1,0:T(8,128)S(1)}, f32[7,1024]{1,0:T(8,128)S(1)}, u32[]{:S(2)}, u32[]{:S(2)}) collective-permute-start(f32[7,1024]{1,0:T(8,128)S(1)} %get-tuple-element.102), channel_id=1, source_target_pairs={{0,7},{1,0},{2,1},{3,2},{4,3},{5,4},{6,5},{7,6},{8,15},{9,8},{10,9... | collective-permute-start | bytes 86024 | tf_op jit(solution)/shard_map/ppermute | solution.py:22
  15.3 2.8 %all-to-all-done = f32[8,4,96]{2,0,1:T(8,128)S(1)} async-done(((f32[8,4,96]{2,0,1:T(8,128)}), f32[8,4,96]{2,0,1:T(8,128)S(1)}, u32[]{:S(2)}, u32[]{:S(2)}) %all-to-all-start) | async-done | bytes 12320 | tf_op jit(solution)/shard_map/all_to_all | solution.py:119
  18.2 0.1 slice.167
  18.2 0.1 slice.169
  18.4 0.1 slice.144
  18.5 0.1 slice.158
  18.5 0.1 slice.161
  18.6 0.1 slice.163
  18.7 0.1 slice.146
  18.8 0.0 collective-permute-done
  18.8 0.1 collective-permute-start.2
  18.9 0.0 collective-permute-done.1
  18.9 2.6 %collective-permute-start.3 = (f32[7,1024]{1,0:T(8,128)S(1)}, f32[7,1024]{1,0:T(8,128)S(1)}, u32[]{:S(2)}, u32[]{:S(2)}) collective-permute-start(f32[7,1024]{1,0:T(8,128)S(1)} %collective-permute-done.1), channel_id=1, source_target_pairs={{0,7},{1,0},{2,1},{3,2},{4,3},{5,4},{6,5},{7,6},{8,15},{9,8},{10,9... | collective-permute-start | bytes 86024 | tf_op jit(solution)/shard_map/ppermute | solution.py:22
  21.5 1.6 %collective-permute-done.2 = f32[7,1024]{1,0:T(8,128)S(1)} collective-permute-done((f32[7,1024]{1,0:T(8,128)S(1)}, f32[7,1024]{1,0:T(8,128)S(1)}, u32[]{:S(2)}, u32[]{:S(2)}) %collective-permute-start.2) | collective-permute-done | bytes 28704 | tf_op jit(solution)/shard_map/ppermute | solution.py:19
  23.1 0.0 collective-permute-start.4
  23.1 0.0 collective-permute-done.3
  23.1 2.6 %collective-permute-start.5 = (f32[7,1024]{1,0:T(8,128)S(1)}, f32[7,1024]{1,0:T(8,128)S(1)}, u32[]{:S(2)}, u32[]{:S(2)}) collective-permute-start(f32[7,1024]{1,0:T(8,128)S(1)} %collective-permute-done.3), channel_id=1, source_target_pairs={{0,7},{1,0},{2,1},{3,2},{4,3},{5,4},{6,5},{7,6},{8,15},{9,8},{10,9... | collective-permute-start | bytes 86024 | tf_op jit(solution)/shard_map/ppermute | solution.py:22
  25.8 1.6 %collective-permute-done.4 = f32[7,1024]{1,0:T(8,128)S(1)} collective-permute-done((f32[7,1024]{1,0:T(8,128)S(1)}, f32[7,1024]{1,0:T(8,128)S(1)}, u32[]{:S(2)}, u32[]{:S(2)}) %collective-permute-start.4) | collective-permute-done | bytes 28704 | tf_op jit(solution)/shard_map/ppermute | solution.py:19
  27.3 0.0 collective-permute-start.6
  27.3 0.0 collective-permute-done.5
  27.4 4.2 %collective-permute-done.6 = f32[7,1024]{1,0:T(8,128)S(1)} collective-permute-done((f32[7,1024]{1,0:T(8,128)S(1)}, f32[7,1024]{1,0:T(8,128)S(1)}, u32[]{:S(2)}, u32[]{:S(2)}) %collective-permute-start.6) | collective-permute-done | bytes 28704 | tf_op jit(solution)/shard_map/ppermute | solution.py:19
  31.6 0.1 fusion.36
  31.6 0.3 fusion.20
  31.9 0.1 maximum_bitcast_fusion
  32.1 0.0 copy-start.3
  32.1 17.6 %while.18 = (s32[]{:T(128)}, f32[6,384]{1,0:T(8,128)S(1)}, f32[4,6,2048]{2,1,0:T(8,128)S(1)}, f32[3,384]{1,0:T(4,128)S(1)}, f32[4,3,2048]{2,1,0:T(4,128)S(1)}, /...) while((s32[]{:T(128)}, f32[6,384]{1,0:T(8,128)S(1)}, ...), condition=%wide.region_4.5_spmd.clone, body=%wide.region_3.4_spmd.clone.sunk | while | flops 65278468 | bytes 200859 | solution.py:71
  32.2 4.3 %fusion.43 = f32[6,384]{1,0:T(8,128)S(1)} fusion(f32[2048]{0:T(1024)S(1)} %bitcast.48, f32[2048]{0:T(1024)S(1)} %bitcast.47, f32[384]{0:T(512)S(1)} %get-tuple-element.161, f32[2048]{0:T(1024)S(1)} %bitcast.46, f32[384]{0:T(512)S(1)} %get-tuple-element.163, f32[2048]{0:T(1024)S(1)} %bitcast.45, f32[384]{0:T(512)S(1)} %get-tuple-element.165, ...), kind=kOutput, calls=%fused_computation.11.clone.1 | convolution fusion | flops 65278464 | bytes 125957 | tf_op jit(solution)/shard_map/while/body/eval_jaxpr/while/body/eval_jaxpr/dot_general | solution.py:66
  36.6 4.3 %fusion.43 = f32[6,384]{1,0:T(8,128)S(1)} fusion(f32[2048]{0:T(1024)S(1)} %bitcast.48, f32[2048]{0:T(1024)S(1)} %bitcast.47, f32[384]{0:T(512)S(1)} %get-tuple-element.161, f32[2048]{0:T(1024)S(1)} %bitcast.46, f32[384]{0:T(512)S(1)} %get-tuple-element.163, f32[2048]{0:T(1024)S(1)} %bitcast.45, f32[384]{0:T(512)S(1)} %get-tuple-element.165, ...), kind=kOutput, calls=%fused_computation.11.clone.1 | convolution fusion | flops 65278464 | bytes 125957 | tf_op jit(solution)/shard_map/while/body/eval_jaxpr/while/body/eval_jaxpr/dot_general | solution.py:66
  41.0 4.3 %fusion.43 = f32[6,384]{1,0:T(8,128)S(1)} fusion(f32[2048]{0:T(1024)S(1)} %bitcast.48, f32[2048]{0:T(1024)S(1)} %bitcast.47, f32[384]{0:T(512)S(1)} %get-tuple-element.161, f32[2048]{0:T(1024)S(1)} %bitcast.46, f32[384]{0:T(512)S(1)} %get-tuple-element.163, f32[2048]{0:T(1024)S(1)} %bitcast.45, f32[384]{0:T(512)S(1)} %get-tuple-element.165, ...), kind=kOutput, calls=%fused_computation.11.clone.1 | convolution fusion | flops 65278464 | bytes 125957 | tf_op jit(solution)/shard_map/while/body/eval_jaxpr/while/body/eval_jaxpr/dot_general | solution.py:66
  45.4 4.3 %fusion.43 = f32[6,384]{1,0:T(8,128)S(1)} fusion(f32[2048]{0:T(1024)S(1)} %bitcast.48, f32[2048]{0:T(1024)S(1)} %bitcast.47, f32[384]{0:T(512)S(1)} %get-tuple-element.161, f32[2048]{0:T(1024)S(1)} %bitcast.46, f32[384]{0:T(512)S(1)} %get-tuple-element.163, f32[2048]{0:T(1024)S(1)} %bitcast.45, f32[384]{0:T(512)S(1)} %get-tuple-element.165, ...), kind=kOutput, calls=%fused_computation.11.clone.1 | convolution fusion | flops 65278464 | bytes 125957 | tf_op jit(solution)/shard_map/while/body/eval_jaxpr/while/body/eval_jaxpr/dot_general | solution.py:66
  49.7 0.0 copy-done.3
  49.7 0.1 multiply_add_fusion
  49.8 0.6 %maximum_multiply_fusion = f32[6,384]{1,0:T(8,128)} fusion(f32[3,384]{1,0:T(4,128)S(1)} %get-tuple-element.98, f32[3,384]{1,0:T(4,128)S(1)} %get-tuple-element.97, f32[384]{0:T(512)S(1)} %slice.167), kind=kLoop, calls=%fused_computation.33 | loop fusion | flops 4608 | bytes 19968 | tf_op jit(solution)/shard_map/mul | solution.py:94
  (41 shorter events, 0.6 us)
Async XLA Ops:
  2.3 10.2 %copy-start = (f32[3,1024]{1,0:T(4,128)S(1)}, f32[3,1024]{1,0:T(4,128)}, u32[]{:S(2)}) copy-start(f32[3,1024]{1,0:T(4,128)} %param.17) | copy-start | bytes 36868
  2.3 10.2 %copy-start.1 = (f32[3,1024]{1,0:T(4,128)S(1)}, f32[3,1024]{1,0:T(4,128)}, u32[]{:S(2)}) copy-start(f32[3,1024]{1,0:T(4,128)} %param.16) | copy-start | bytes 36868
  2.3 10.2 %copy-start.2 = (f32[1024]{0:T(1024)S(1)}, f32[1024]{0:T(1024)}, u32[]{:S(2)}) copy-start(f32[1024]{0:T(1024)} %param.18) | copy-start | bytes 12292
  6.2 11.9 %all-to-all-start = ((f32[8,4,96]{2,0,1:T(8,128)}), f32[8,4,96]{2,0,1:T(8,128)S(1)}, u32[]{:S(2)}, u32[]{:S(2)}) async-start(f32[8,4,96]{2,0,1:T(8,128)} %copy.17), calls=%async_computation | async-start | bytes 32768 | tf_op jit(solution)/shard_map/all_to_all | solution.py:119
  12.6 6.2 %collective-permute-start = (f32[7,1024]{1,0:T(8,128)S(1)}, f32[7,1024]{1,0:T(8,128)S(1)}, u32[]{:S(2)}, u32[]{:S(2)}) collective-permute-start(f32[7,1024]{1,0:T(8,128)S(1)} %get-tuple-element.102), channel_id=1, source_target_pairs={{0,1},{1,2},{2,3},{3,4},{4,5},{5,6},{6,7},{7,0},{8,9},{9,10},{10,1... | collective-permute-start | bytes 86024 | tf_op jit(solution)/shard_map/ppermute | solution.py:19
  12.6 6.2 %collective-permute-start.1 = (f32[7,1024]{1,0:T(8,128)S(1)}, f32[7,1024]{1,0:T(8,128)S(1)}, u32[]{:S(2)}, u32[]{:S(2)}) collective-permute-start(f32[7,1024]{1,0:T(8,128)S(1)} %get-tuple-element.102), channel_id=1, source_target_pairs={{0,7},{1,0},{2,1},{3,2},{4,3},{5,4},{6,5},{7,6},{8,15},{9,8},{10,9... | collective-permute-start | bytes 86024 | tf_op jit(solution)/shard_map/ppermute | solution.py:22
  18.8 4.3 %collective-permute-start.2 = (f32[7,1024]{1,0:T(8,128)S(1)}, f32[7,1024]{1,0:T(8,128)S(1)}, u32[]{:S(2)}, u32[]{:S(2)}) collective-permute-start(f32[7,1024]{1,0:T(8,128)S(1)} %collective-permute-done), channel_id=1, source_target_pairs={{0,1},{1,2},{2,3},{3,4},{4,5},{5,6},{6,7},{7,0},{8,9},{9,10},{10,1... | collective-permute-start | bytes 86024 | tf_op jit(solution)/shard_map/ppermute | solution.py:19
  18.9 4.2 %collective-permute-start.3 = (f32[7,1024]{1,0:T(8,128)S(1)}, f32[7,1024]{1,0:T(8,128)S(1)}, u32[]{:S(2)}, u32[]{:S(2)}) collective-permute-start(f32[7,1024]{1,0:T(8,128)S(1)} %collective-permute-done.1), channel_id=1, source_target_pairs={{0,7},{1,0},{2,1},{3,2},{4,3},{5,4},{6,5},{7,6},{8,15},{9,8},{10,9... | collective-permute-start | bytes 86024 | tf_op jit(solution)/shard_map/ppermute | solution.py:22
  23.1 4.2 %collective-permute-start.4 = (f32[7,1024]{1,0:T(8,128)S(1)}, f32[7,1024]{1,0:T(8,128)S(1)}, u32[]{:S(2)}, u32[]{:S(2)}) collective-permute-start(f32[7,1024]{1,0:T(8,128)S(1)} %collective-permute-done.2), channel_id=1, source_target_pairs={{0,1},{1,2},{2,3},{3,4},{4,5},{5,6},{6,7},{7,0},{8,9},{9,10},{10,1... | collective-permute-start | bytes 86024 | tf_op jit(solution)/shard_map/ppermute | solution.py:19
  23.1 4.2 %collective-permute-start.5 = (f32[7,1024]{1,0:T(8,128)S(1)}, f32[7,1024]{1,0:T(8,128)S(1)}, u32[]{:S(2)}, u32[]{:S(2)}) collective-permute-start(f32[7,1024]{1,0:T(8,128)S(1)} %collective-permute-done.3), channel_id=1, source_target_pairs={{0,7},{1,0},{2,1},{3,2},{4,3},{5,4},{6,5},{7,6},{8,15},{9,8},{10,9... | collective-permute-start | bytes 86024 | tf_op jit(solution)/shard_map/ppermute | solution.py:22
  27.3 4.2 %collective-permute-start.6 = (f32[7,1024]{1,0:T(8,128)S(1)}, f32[7,1024]{1,0:T(8,128)S(1)}, u32[]{:S(2)}, u32[]{:S(2)}) collective-permute-start(f32[7,1024]{1,0:T(8,128)S(1)} %collective-permute-done.4), channel_id=1, source_target_pairs={{0,1},{1,2},{2,3},{3,4},{4,5},{5,6},{6,7},{7,0},{8,9},{9,10},{10,1... | collective-permute-start | bytes 86024 | tf_op jit(solution)/shard_map/ppermute | solution.py:19
  32.1 17.6 %copy-start.3 = (f32[3]{0:T(128)S(1)}, f32[3]{0:T(128)}, u32[]{:S(2)}) copy-start(f32[3]{0:T(128)} %constant.116) | copy-start | bytes 40
